TPU v7x, 512 devices: a whole 4x8x8 slice. The times are simulated.
512 devices in a mesh: group: 8 (over x, y_hi), sub: 64 (over y_lo, z, core).
Axes of the slice: x: 4, y: 8 (y_hi: 2, y_lo: 4; y = y_hi * 4 + y_lo), z: 8, core: 2. Of those that a mesh axis runs over, the one named last changes fastest.
Arguments:
- modes: bfloat16 [524288, 512], P(('group', 'sub')), may hold values from -6 to 6
- block_vals: bfloat16 [24576, 128, 128], P(('group', 'sub')), may hold values from -0.21875 to 0.21875
- block_cols: int32 [24576], P(('group', 'sub')), may hold values from 0 to 7, as said below
- level_maps: bfloat16 [2, 128, 128], replicated, may hold values from -0.5 to 0.5
- psi: bfloat16 [524288, 512], P(('group', 'sub')), may hold values from -0.09375 to 0.09375
- parent_vals: bfloat16 [4096, 128, 128], P(('group', 'sub')), may hold values from -0.09375 to 0.09375
- parent_rows: int32 [4096], P(('group', 'sub')), may hold values from 0 to 63
Outputs:
- parent_coupling: bfloat16 [8192, 1024], P('sub', 'group')
- projected: float32 [4096, 512], P(('group', 'sub'))
Inputs may be any that keep to these rules, and one draw needn't show every extreme that they name: `block_cols`: within one interface row block of one device the 6 vertex blocks are distinct.
All inputs are finite; a program needn't handle non-finite values.
Results may differ from a plain program's by a relative error of at most 0.0078.
Values may be sent and summed in bfloat16 or wider, within the bound.
No kernel may reach another device: no remote copies, remote signals or barrier semaphores. Data moves between devices by JAX's collectives and lax.ppermute only.
A program may use at most 64 MiB of HBM per device.

v0:
```python
import jax
import jax.numpy as jnp
from jax import lax
from jax.sharding import PartitionSpec as P

IFB = 8
BPR = 6


def from_partner(value, axis, distance):
    mask = 2**distance
    pairs = [(source, source ^ mask) for source in range(lax.axis_size(axis))]
    return lax.ppermute(value, axis, pairs)


def on_device(modes, block_vals, block_cols, level_maps, psi, parent_vals, parent_rows):
    block_size = block_vals.shape[1]
    width = modes.shape[1]
    vertex_blocks = modes.shape[0] // block_size
    row_blocks = IFB
    levels = min(2, lax.axis_size("group").bit_length() - 1)
    group_index = lax.axis_index("group")
    onehot = (
        block_cols.reshape(row_blocks, BPR)[:, :, None] == jnp.arange(vertex_blocks)[None, None, :]
    ).astype(jnp.float32)
    blocks = block_vals.astype(jnp.float32).reshape(row_blocks, BPR, block_size, block_size)
    dense = (
        jnp.einsum("rbc,rbij->ricj", onehot, blocks)
        .reshape(row_blocks * block_size, vertex_blocks * block_size)
        .astype(jnp.bfloat16)
    )
    panel = jnp.dot(dense, modes, preferred_element_type=jnp.float32).astype(jnp.bfloat16)
    for level in range(levels):
        sibling = from_partner(panel, "group", level)
        total = (panel.astype(jnp.float32) + sibling.astype(jnp.float32)).astype(jnp.bfloat16)
        mapped = jnp.einsum(
            "ab,rbm->ram",
            level_maps[level],
            total.reshape(row_blocks, block_size, width),
            preferred_element_type=jnp.float32,
        )
        panel = mapped.reshape(row_blocks * block_size, width).astype(jnp.bfloat16)
    head = panel[:block_size]
    piece = lax.all_gather(head, "sub", axis=0, tiled=True)
    owners_here = piece.shape[0] // block_size
    owners = jnp.arange(owners_here)
    select = (parent_rows[:, None] == owners[None, :]).astype(jnp.bfloat16)
    picked = jnp.einsum(
        "kj,jbm->kbm",
        select,
        piece.reshape(owners_here, block_size, width),
        preferred_element_type=jnp.float32,
    ).astype(jnp.bfloat16)
    partial_sum = jnp.einsum("kab,kbm->am", parent_vals, picked, preferred_element_type=jnp.float32)
    for level in reversed(range(levels)):
        half = partial_sum.shape[1] // 2
        upper = group_index >> level & 1
        keeper = lax.dynamic_slice_in_dim(partial_sum, upper * half, half, 1)
        sender = lax.dynamic_slice_in_dim(partial_sum, (1 - upper) * half, half, 1)
        partial_sum = keeper + from_partner(sender, "group", level)
    parent_out = partial_sum.astype(jnp.bfloat16)
    projected = lax.psum_scatter(
        lax.dot_general(psi, panel, (((0,), (0,)), ((), ())), preferred_element_type=jnp.float32),
        "sub",
        scatter_dimension=0,
        tiled=True,
    )
    return (parent_out, projected)


def solution(mesh):
    return jax.shard_map(
        on_device,
        mesh=mesh,
        in_specs=(
            P(("group", "sub"), None),
            P(("group", "sub"), None, None),
            P(("group", "sub")),
            P(),
            P(("group", "sub"), None),
            P(("group", "sub"), None, None),
            P(("group", "sub")),
        ),
        out_specs=(P("sub", "group"), P(("group", "sub"), None)),
        check_vma=False,
    )
```

profile of v0, /device:TPU:2, one launch (start us, length us, event | category | flops | bytes accessed | tf_op | source)
XLA Modules:
  0.0 514.9 jit_solution(13691395936488366939)
XLA Ops:
  7.2 0.0 copy-start
  7.2 0.0 all-gather.3.cloned.1.call-start
  7.2 0.8 eq.31
  8.1 0.5 copy-done
  8.6 0.0 copy-start.4
  8.6 1.0 fusion.7
  9.6 0.2 copy-done.4
  9.8 1.2 fusion.10
  11.1 0.0 copy-start.2
  11.1 7.9 %collective-permute-start = (bf16[1024,512]{1,0:T(8,128)(2,1)S(1)}, bf16[1024,512]{1,0:T(8,128)(2,1)S(1)}, u32[]{:S(2)}, u32[]{:S(2)}) collective-permute-start(bf16[1024,512]{1,0:T(8,128)(2,1)S(1)} %fusion.10), channel_id=1, source_target_pairs={{0,64},{64,0},{128,192},{192,128},{256,320},{320,256},{384,448},{4... | collective-permute-start | bytes 3145736 | tf_op jit(solution)/shard_map/ppermute | solution.py:13
  19.0 45.1 %collective-permute-done = bf16[1024,512]{1,0:T(8,128)(2,1)S(1)} collective-permute-done((bf16[1024,512]{1,0:T(8,128)(2,1)S(1)}, bf16[1024,512]{1,0:T(8,128)(2,1)S(1)}, u32[]{:S(2)}, u32[]{:S(2)}) %collective-permute-start) | collective-permute-done | bytes 1048608 | tf_op jit(solution)/shard_map/ppermute | solution.py:13
  64.0 0.3 add_convert_fusion.1
  64.4 0.0 copy-done.2
  64.4 0.4 convolution_convert_fusion.1
  64.8 2.4 collective-permute-start.1
  67.2 14.2 %collective-permute-done.1 = bf16[1024,512]{1,0:T(8,128)(2,1)S(1)} collective-permute-done((bf16[1024,512]{1,0:T(8,128)(2,1)S(1)}, bf16[1024,512]{1,0:T(8,128)(2,1)S(1)}, u32[]{:S(2)}, u32[]{:S(2)}) %collective-permute-start.1) | collective-permute-done | bytes 1048608 | tf_op jit(solution)/shard_map/ppermute | solution.py:13
  81.5 0.4 add_convert_fusion
  81.9 0.4 convolution_convert_fusion
  82.3 0.7 slice.16
  82.9 0.0 all-gather.3.cloned.1.call-update
  83.0 0.2 reduce-scatter.4.cloned.1.call-start
  83.2 2.9 convolution_bitcast_fusion
  86.1 0.0 copy-start.3
  86.1 2.6 copy.18
  88.7 0.0 reduce-scatter.4.cloned.1.call-update
  88.8 130.8 %all-gather.3.cloned.1.call-done = bf16[1,8192,512]{2,1,0:T(8,128)(2,1)} async-done(((bf16[1,128,512]{2,1,0:T(8,128)(2,1)}), bf16[1,8192,512]{2,1,0:T(8,128)(2,1)}) %all-gather.3.cloned.1.call-update) | async-done | bytes 8388624 | tf_op jit(solution)/shard_map/all_gather | solution.py:44
  219.6 0.0 copy-done.3
  219.6 12.2 %fusion = bf16[8,128,512]{2,0,1:T(8,128)(2,1)S(1)} fusion(bf16[64,128,512]{2,1,0:T(8,128)(2,1)} %bitcast.52, s32[8]{0:T(128)S(1)} %copy-done.3), kind=kOutput, calls=%fused_computation | convolution fusion | flops 67109376 | bytes 9437216 | tf_op jit(solution)/shard_map/kj,jbm->kbm/dot_general | solution.py:48
  231.8 0.0 copy-start.1
  231.8 1.7 copy.17
  233.5 0.0 copy-done.1
  233.5 1.7 convolution_bitcast_fusion.1
  235.2 2.5 collective-permute-start.2
  237.7 5.0 collective-permute-done.2
  242.8 8.1 %collective-permute-start.3 = (f32[128,128]{0,1:T(8,128)S(1)}, f32[128,128]{0,1:T(8,128)S(1)}, u32[]{:S(2)}, u32[]{:S(2)}) collective-permute-start(f32[128,128]{0,1:T(8,128)S(1)} %constant_dynamic-slice_fusion), channel_id=1, source_target_pairs={{0,64},{64,0},{128,192},{192,128},{256,320},{320,256},{384,448},{4... | collective-permute-start | bytes 196616 | tf_op jit(solution)/shard_map/ppermute | solution.py:13
  250.8 2.2 collective-permute-done.3
  253.1 0.7 copy.13
  253.8 254.3 %reduce-scatter.4.cloned.1.call-done = f32[8,512]{1,0:T(8,128)} async-done(((f32[512,512]{1,0:T(8,128)}), f32[8,512]{1,0:T(8,128)}) %reduce-scatter.4.cloned.1.call-update) | async-done | bytes 16400
  (4 shorter events, 0.1 us)
Async XLA Ops:
  7.2 1.4 copy-start
  7.2 212.4 %all-gather.3.cloned.1.call-start = ((), (), s32[]{:S(2)}) async-start(), calls=%async_computation.1 | async-start | bytes 8519680 | tf_op jit(solution)/shard_map/all_gather | solution.py:44
  8.6 1.2 copy-start.4
  11.1 53.3 %copy-start.2 = (bf16[2,128,128]{2,1,0:T(8,128)(2,1)S(1)}, bf16[2,128,128]{2,1,0:T(8,128)(2,1)}, u32[]{:S(2)}) copy-start(bf16[2,128,128]{2,1,0:T(8,128)(2,1)} %param.10) | copy-start | bytes 196612
  11.1 53.0 %collective-permute-start = (bf16[1024,512]{1,0:T(8,128)(2,1)S(1)}, bf16[1024,512]{1,0:T(8,128)(2,1)S(1)}, u32[]{:S(2)}, u32[]{:S(2)}) collective-permute-start(bf16[1024,512]{1,0:T(8,128)(2,1)S(1)} %fusion.10), channel_id=1, source_target_pairs={{0,64},{64,0},{128,192},{192,128},{256,320},{320,256},{384,448},{4... | collective-permute-start | bytes 3145736 | tf_op jit(solution)/shard_map/ppermute | solution.py:13
  64.8 16.7 %collective-permute-start.1 = (bf16[1024,512]{1,0:T(8,128)(2,1)S(1)}, bf16[1024,512]{1,0:T(8,128)(2,1)S(1)}, u32[]{:S(2)}, u32[]{:S(2)}) collective-permute-start(bf16[1024,512]{1,0:T(8,128)(2,1)S(1)} %bitcast.53), channel_id=1, source_target_pairs={{0,128},{64,192},{128,0},{192,64},{256,384},{320,448},{384,256},{4... | collective-permute-start | bytes 3145736 | tf_op jit(solution)/shard_map/ppermute | solution.py:13
  83.0 425.1 %reduce-scatter.4.cloned.1.call-start = ((), (), s32[]{:S(2)}) async-start(), calls=%async_computation.2 | async-start | bytes 1064960
  86.1 133.4 %copy-start.3 = (s32[8]{0:T(128)S(1)}, s32[8]{0:T(128)}, u32[]{:S(2)}) copy-start(s32[8]{0:T(128)} %param.13) | copy-start | bytes 100
  231.8 1.7 copy-start.1
  235.2 7.5 %collective-permute-start.2 = (f32[128,256]{0,1:T(8,128)S(1)}, f32[128,256]{0,1:T(8,128)S(1)}, u32[]{:S(2)}, u32[]{:S(2)}) collective-permute-start(f32[128,256]{0,1:T(8,128)S(1)} %dynamic-slice_bitcast_fusion), channel_id=1, source_target_pairs={{0,128},{64,192},{128,0},{192,64},{256,384},{320,448},{384,256},{4... | collective-permute-start | bytes 393224 | tf_op jit(solution)/shard_map/ppermute | solution.py:13
  242.8 10.3 %collective-permute-start.3 = (f32[128,128]{0,1:T(8,128)S(1)}, f32[128,128]{0,1:T(8,128)S(1)}, u32[]{:S(2)}, u32[]{:S(2)}) collective-permute-start(f32[128,128]{0,1:T(8,128)S(1)} %constant_dynamic-slice_fusion), channel_id=1, source_target_pairs={{0,64},{64,0},{128,192},{192,128},{256,320},{320,256},{384,448},{4... | collective-permute-start | bytes 196616 | tf_op jit(solution)/shard_map/ppermute | solution.py:13
Sparse Core Ops, SparseCore 0:
  83.1 136.4 all-gather.2
  222.9 285.1 reduce-scatter.3
where the time goes:
time: 515 us
  waiting for transfers between devices  452 us (88%)
  starting transfers between devices  21.1 us (4%)
  matrix products  19.9 us (4%)
  between operations  14.2 us (3%)
  local copies, waits for them, and re-layouts  7.35 us (1%)
    unnamed x3, waiting for transfers between devices  254 us
    all_gather x1, waiting for transfers between devices, on_device(): piece = lax.all_gather(head, 'sub', axis=0, tiled=True)  131 us
    ppermute x4, waiting for transfers between devices, from_partner(): return lax.ppermute(value, axis, pairs)  66.6 us
    ppermute x4, starting transfers between devices, from_partner(): return lax.ppermute(value, axis, pairs)  20.8 us
    dot_general x1, matrix products, on_device(): jnp.einsum('kj,jbm->kbm', select, piece.reshape(owners_here, block_size,...  12.2 us
  transfers between devices with their start and end apart: 6, of which 6 were waited for; matrix products, arithmetic and copies ran while one was open for 4% of the time, Pallas kernels for 0%

commit v1 on v0

--- a/solution.py
+++ b/solution.py
@@ -41,7 +41,9 @@
         )
         panel = mapped.reshape(row_blocks * block_size, width).astype(jnp.bfloat16)
     head = panel[:block_size]
-    piece = lax.all_gather(head, "sub", axis=0, tiled=True)
+    piece = jnp.concatenate(
+        lax.all_to_all(jnp.stack([head] * lax.axis_size("sub")), "sub", 0, 0), axis=0
+    )
     owners_here = piece.shape[0] // block_size
     owners = jnp.arange(owners_here)
     select = (parent_rows[:, None] == owners[None, :]).astype(jnp.bfloat16)

time: 515 us -> 556 us (1.080)
  the two profiles are of different devices: /device:TPU:2 before, /device:TPU:4 now
where the time goes in v1:
time: 556 us; the launch traced here: 555 us
  waiting for transfers between devices  454 us (82%)
  starting transfers between devices  55.9 us (10%)
  matrix products  20 us (4%)
  between operations  14.2 us (3%)
  local copies, waits for them, and re-layouts  10.9 us (2%)
    all_to_all x1, waiting for transfers between devices, on_device(): lax.all_to_all(jnp.stack([head] * lax.axis_size('sub')), 'sub', 0, 0)  215 us
    unnamed x2, waiting for transfers between devices  173 us
    ppermute x4, waiting for transfers between devices, from_partner(): return lax.ppermute(value, axis, pairs)  65.8 us
    ppermute x4, starting transfers between devices, from_partner(): return lax.ppermute(value, axis, pairs)  31.5 us
    all_to_all x1, starting transfers between devices, on_device(): lax.all_to_all(jnp.stack([head] * lax.axis_size('sub')), 'sub', 0, 0)  24.2 us
    dot_general x1, matrix products, on_device(): jnp.einsum('kj,jbm->kbm', select, piece.reshape(owners_here, block_size,...  12.2 us
  transfers between devices with their start and end apart: 6, of which 6 were waited for; matrix products, arithmetic and copies ran while one was open for 4% of the time, Pallas kernels for 0%

profile of v1, /device:TPU:4, one launch (start us, length us, event | category | flops | bytes accessed | tf_op | source)
XLA Modules:
  0.0 555.2 jit_solution(11249220287774609341)
XLA Ops:
  7.2 0.0 copy-start
  7.2 0.8 eq.31
  8.0 0.6 copy-done
  8.6 0.0 copy-start.4
  8.6 1.0 fusion.7
  9.6 0.2 copy-done.4
  9.8 1.2 fusion.10
  11.1 0.0 copy-start.2
  11.1 7.9 %collective-permute-start = (bf16[1024,512]{1,0:T(8,128)(2,1)S(1)}, bf16[1024,512]{1,0:T(8,128)(2,1)S(1)}, u32[]{:S(2)}, u32[]{:S(2)}) collective-permute-start(bf16[1024,512]{1,0:T(8,128)(2,1)S(1)} %fusion.10), channel_id=1, source_target_pairs={{0,64},{64,0},{128,192},{192,128},{256,320},{320,256},{384,448},{4... | collective-permute-start | bytes 3145736 | tf_op jit(solution)/shard_map/ppermute | solution.py:13
  18.9 45.1 %collective-permute-done = bf16[1024,512]{1,0:T(8,128)(2,1)S(1)} collective-permute-done((bf16[1024,512]{1,0:T(8,128)(2,1)S(1)}, bf16[1024,512]{1,0:T(8,128)(2,1)S(1)}, u32[]{:S(2)}, u32[]{:S(2)}) %collective-permute-start) | collective-permute-done | bytes 1048608 | tf_op jit(solution)/shard_map/ppermute | solution.py:13
  64.0 0.3 add_convert_fusion.1
  64.4 0.0 copy-done.2
  64.4 0.4 convolution_convert_fusion.1
  64.8 3.1 collective-permute-start.1
  67.9 13.6 %collective-permute-done.1 = bf16[1024,512]{1,0:T(8,128)(2,1)S(1)} collective-permute-done((bf16[1024,512]{1,0:T(8,128)(2,1)S(1)}, bf16[1024,512]{1,0:T(8,128)(2,1)S(1)}, u32[]{:S(2)}, u32[]{:S(2)}) %collective-permute-start.1) | collective-permute-done | bytes 1048608 | tf_op jit(solution)/shard_map/ppermute | solution.py:13
  81.5 0.4 add_convert_fusion
  81.9 0.4 convolution_convert_fusion
  82.3 4.3 stack.2
  86.6 24.2 %all-to-all-start = ((bf16[64,128,512]{2,1,0:T(8,128)(2,1)}), bf16[64,128,512]{2,1,0:T(8,128)(2,1)}, u32[]{:S(2)}, u32[]{:S(2)}) async-start(bf16[64,128,512]{2,1,0:T(8,128)(2,1)} %stack.2), calls=%async_computation | async-start | bytes 16777216 | tf_op jit(solution)/shard_map/all_to_all | solution.py:45
  110.8 0.2 reduce-scatter.4.cloned.1.call-start
  111.0 3.0 convolution_bitcast_fusion
  114.0 0.0 copy-start.3
  114.0 2.6 copy.18
  116.5 0.0 reduce-scatter.4.cloned.1.call-update
  116.6 215.0 %all-to-all-done = bf16[64,128,512]{2,1,0:T(8,128)(2,1)} async-done(((bf16[64,128,512]{2,1,0:T(8,128)(2,1)}), bf16[64,128,512]{2,1,0:T(8,128)(2,1)}, u32[]{:S(2)}, u32[]{:S(2)}) %all-to-all-start) | async-done | bytes 8388640 | tf_op jit(solution)/shard_map/all_to_all | solution.py:45
  331.6 0.0 copy-done.3
  331.6 12.2 %fusion = bf16[8,128,512]{2,0,1:T(8,128)(2,1)S(1)} fusion(bf16[64,128,512]{2,1,0:T(8,128)(2,1)} %all-to-all-done, s32[8]{0:T(128)S(1)} %copy-done.3), kind=kOutput, calls=%fused_computation | convolution fusion | flops 67109376 | bytes 9437216 | tf_op jit(solution)/shard_map/kj,jbm->kbm/dot_general | solution.py:50
  343.9 0.0 copy-start.1
  343.9 1.7 copy.17
  345.6 0.0 copy-done.1
  345.6 1.7 convolution_bitcast_fusion.1
  347.2 1.9 collective-permute-start.2
  349.2 4.9 collective-permute-done.2
  354.1 18.6 %collective-permute-start.3 = (f32[128,128]{0,1:T(8,128)S(1)}, f32[128,128]{0,1:T(8,128)S(1)}, u32[]{:S(2)}, u32[]{:S(2)}) collective-permute-start(f32[128,128]{0,1:T(8,128)S(1)} %constant_dynamic-slice_fusion), channel_id=1, source_target_pairs={{0,64},{64,0},{128,192},{192,128},{256,320},{320,256},{384,448},{4... | collective-permute-start | bytes 196616 | tf_op jit(solution)/shard_map/ppermute | solution.py:13
  372.7 2.2 collective-permute-done.3
  375.0 0.7 copy.13
  375.7 172.6 %reduce-scatter.4.cloned.1.call-done = f32[8,512]{1,0:T(8,128)} async-done(((f32[512,512]{1,0:T(8,128)}), f32[8,512]{1,0:T(8,128)}) %reduce-scatter.4.cloned.1.call-update) | async-done | bytes 16400
  (5 shorter events, 0.1 us)
Async XLA Ops:
  7.2 1.4 copy-start
  8.6 1.2 copy-start.4
  11.1 53.3 %copy-start.2 = (bf16[2,128,128]{2,1,0:T(8,128)(2,1)S(1)}, bf16[2,128,128]{2,1,0:T(8,128)(2,1)}, u32[]{:S(2)}) copy-start(bf16[2,128,128]{2,1,0:T(8,128)(2,1)} %param.10) | copy-start | bytes 196612
  11.1 53.0 %collective-permute-start = (bf16[1024,512]{1,0:T(8,128)(2,1)S(1)}, bf16[1024,512]{1,0:T(8,128)(2,1)S(1)}, u32[]{:S(2)}, u32[]{:S(2)}) collective-permute-start(bf16[1024,512]{1,0:T(8,128)(2,1)S(1)} %fusion.10), channel_id=1, source_target_pairs={{0,64},{64,0},{128,192},{192,128},{256,320},{320,256},{384,448},{4... | collective-permute-start | bytes 3145736 | tf_op jit(solution)/shard_map/ppermute | solution.py:13
  64.8 16.7 %collective-permute-start.1 = (bf16[1024,512]{1,0:T(8,128)(2,1)S(1)}, bf16[1024,512]{1,0:T(8,128)(2,1)S(1)}, u32[]{:S(2)}, u32[]{:S(2)}) collective-permute-start(bf16[1024,512]{1,0:T(8,128)(2,1)S(1)} %bitcast.53), channel_id=1, source_target_pairs={{0,128},{64,192},{128,0},{192,64},{256,384},{320,448},{384,256},{4... | collective-permute-start | bytes 3145736 | tf_op jit(solution)/shard_map/ppermute | solution.py:13
  86.6 245.0 %all-to-all-start = ((bf16[64,128,512]{2,1,0:T(8,128)(2,1)}), bf16[64,128,512]{2,1,0:T(8,128)(2,1)}, u32[]{:S(2)}, u32[]{:S(2)}) async-start(bf16[64,128,512]{2,1,0:T(8,128)(2,1)} %stack.2), calls=%async_computation | async-start | bytes 16777216 | tf_op jit(solution)/shard_map/all_to_all | solution.py:45
  110.8 437.6 %reduce-scatter.4.cloned.1.call-start = ((), (), s32[]{:S(2)}) async-start(), calls=%async_computation.2 | async-start | bytes 1064960
  114.0 217.6 %copy-start.3 = (s32[8]{0:T(128)S(1)}, s32[8]{0:T(128)}, u32[]{:S(2)}) copy-start(s32[8]{0:T(128)} %param.13) | copy-start | bytes 100
  343.9 1.7 copy-start.1
  347.2 6.9 %collective-permute-start.2 = (f32[128,256]{0,1:T(8,128)S(1)}, f32[128,256]{0,1:T(8,128)S(1)}, u32[]{:S(2)}, u32[]{:S(2)}) collective-permute-start(f32[128,256]{0,1:T(8,128)S(1)} %dynamic-slice_bitcast_fusion), channel_id=1, source_target_pairs={{0,128},{64,192},{128,0},{192,64},{256,384},{320,448},{384,256},{4... | collective-permute-start | bytes 393224 | tf_op jit(solution)/shard_map/ppermute | solution.py:13
  354.1 20.8 %collective-permute-start.3 = (f32[128,128]{0,1:T(8,128)S(1)}, f32[128,128]{0,1:T(8,128)S(1)}, u32[]{:S(2)}, u32[]{:S(2)}) collective-permute-start(f32[128,128]{0,1:T(8,128)S(1)} %constant_dynamic-slice_fusion), channel_id=1, source_target_pairs={{0,64},{64,0},{128,192},{192,128},{256,320},{320,256},{384,448},{4... | collective-permute-start | bytes 196616 | tf_op jit(solution)/shard_map/ppermute | solution.py:13
Sparse Core Ops, SparseCore 0:
  116.7 431.6 reduce-scatter.3
